TPU v7x, 512 devices: a whole 4x8x8 slice. The times are simulated.
512 devices in a mesh: sub: 8 (over x, core), seq: 8 (over y), exp: 8 (over z).
Axes of the slice: x: 4, y: 8, z: 8, core: 2. Of those that a mesh axis runs over, the one named last changes fastest.
Arguments:
- node_features: bfloat16 [64, 1536, 1024], P(('sub', 'exp'), 'seq'), parts along dimension 0, may hold values from -24 to 24
- block_mask: int32 [64, 12, 12], P(('sub', 'exp')), parts along dimension 0, may hold values from 0 to 1, as said below
- w_qkv: bfloat16 [1024, 3072], P('exp', 'seq'), may hold values from -4 to 4
- w_out: bfloat16 [1024, 1024], P('seq', 'exp'), may hold values from -0.1875 to 0.1875
- norm_gain: float32 [1024], replicated, may hold values from 0.5 to 1.5
- routes: int32 [64, 1536, 2], P(('sub', 'exp'), 'seq'), parts along dimension 0, may hold values from 0 to 63, all different within a row; in each aligned block of 192 rows (0 to 191, 192 to 383, ..., all dimensions but the last counted through in order) at most 12 rows name the same one
- gates: float32 [64, 1536, 2], P(('sub', 'exp'), 'seq'), parts along dimension 0, may hold values from 0.1 to 1
- w_gate_up: bfloat16 [64, 1024, 1024], P(('seq', 'exp')), may hold values from -0.1875 to 0.1875
- w_down: bfloat16 [64, 512, 1024], P(('seq', 'exp')), may hold values from -0.25 to 0.25
Outputs:
- layer_out: bfloat16 [64, 1536, 1024], P(('sub', 'exp'), 'seq'), parts along dimension 0
There are 8 independent parts, one for each index of `sub`. A program takes and returns all parts, laid end to end along the dimension named above; an argument that names none is the same for every part. Nothing has to cross between parts.
Inputs may be any that keep to these rules, and one draw needn't show every extreme that they name: In each aligned block of 192 rows (one device's nodes, subgraphs then nodes in order) no expert is named by more than 12 of the rows' routes, a bound that some block reaches; the 2 experts of a node differ. `block_mask`: the diagonal blocks are 1.
All inputs are finite; a program needn't handle non-finite values.
Results may differ from a plain program's by a relative error of at most 0.0065.
The roundings to bfloat16 on the way count: a program that leaves them out, or rounds other values in their place, can miss the bound.
Values may be sent and summed in bfloat16 or wider, within the bound.
No kernel may reach another device: no remote copies, remote signals or barrier semaphores. Data moves between devices by JAX's collectives and lax.ppermute only.
A program may use at most 64 MiB of HBM per device.

v0:
```python
import math
import jax
import jax.numpy as jnp
from jax import lax
from jax.sharding import PartitionSpec as P

HEAD_DIM = 64
TOP = 2
BLOCK = 128


def per_device(
    node_features, block_mask, w_qkv, w_out, norm_gain, routes, gates, w_gate_up, w_down
):
    feats = node_features[0]
    node_dev, width = feats.shape
    seq_count = lax.axis_size("seq")
    exp_count = lax.axis_size("exp")
    experts = seq_count * exp_count * w_gate_up.shape[0]
    head_cols = w_qkv.shape[1]
    qkv_all, out_all = (
        lax.all_gather(w_qkv[None], ("seq", "exp"), axis=0, tiled=True),
        lax.all_gather(w_out[None], ("seq", "exp"), axis=0, tiled=True),
    )
    qkv_tiles = qkv_all.reshape(seq_count, exp_count, w_qkv.shape[0], head_cols)
    local_proj = jnp.einsum(
        "nek,sekc->nsc",
        feats.reshape(node_dev, exp_count, w_qkv.shape[0]),
        qkv_tiles,
        preferred_element_type=jnp.float32,
    )
    local_proj = local_proj.astype(jnp.bfloat16).reshape(node_dev, seq_count * head_cols)
    projected = lax.all_to_all(local_proj, "seq", split_axis=1, concat_axis=0, tiled=True)
    nodes = projected.shape[0]
    heads_here = head_cols // (3 * HEAD_DIM)
    split = projected.reshape(nodes, heads_here, 3, HEAD_DIM)
    query = split[:, :, 0]
    keys = split[:, :, 1]
    values = split[:, :, 2]
    col_mask = jnp.repeat(block_mask[0], BLOCK, axis=1) > 0
    span = math.gcd(nodes, 512)
    scale = 1.0 / math.sqrt(HEAD_DIM)

    def attend(index):
        start = index * span
        rows_query = lax.dynamic_slice_in_dim(query, start, span, 0)
        rows_mask = lax.dynamic_slice_in_dim(col_mask, start // BLOCK, span // BLOCK, 0)
        allowed = jnp.repeat(rows_mask, BLOCK, axis=0)
        scores = (
            jnp.einsum("qhd,khd->hqk", rows_query, keys, preferred_element_type=jnp.float32) * scale
        )
        scores = jnp.where(allowed[None], scores, -1e30)
        top = jnp.max(scores, axis=-1, keepdims=True)
        weights = jnp.exp(scores - top)
        probs = (weights / jnp.sum(weights, axis=-1, keepdims=True)).astype(jnp.bfloat16)
        return jnp.einsum("hqk,khd->qhd", probs, values, preferred_element_type=jnp.float32).astype(
            jnp.bfloat16
        )

    blocks = lax.map(attend, jnp.arange(nodes // span, dtype=jnp.int32))
    attended = blocks.reshape(nodes, heads_here * HEAD_DIM)
    node_attended = lax.all_to_all(attended, "seq", split_axis=0, concat_axis=1, tiled=True)
    out_tiles = out_all.reshape(seq_count, exp_count, w_out.shape[0], w_out.shape[1])
    attn_out = jnp.einsum(
        "nsk,sekc->nec",
        node_attended.reshape(node_dev, seq_count, w_out.shape[0]),
        out_tiles,
        preferred_element_type=jnp.float32,
    )
    mixed = feats.astype(jnp.float32) + attn_out.reshape(node_dev, width)
    mean_square = jnp.mean(mixed * mixed, axis=-1, keepdims=True)
    normed = (mixed * lax.rsqrt(mean_square + 1e-06) * norm_gain).astype(jnp.bfloat16)
    capacity = 2 * TOP * node_dev // experts
    pair_routes = routes[0].reshape(node_dev * TOP)
    onehot = (pair_routes[:, None] == jnp.arange(experts, dtype=jnp.int32)).astype(jnp.int32)
    earlier = jnp.cumsum(onehot, axis=0, dtype=jnp.int32) - onehot
    slots = jnp.sum(earlier * onehot, axis=1, dtype=jnp.int32)
    position = pair_routes * capacity + slots
    outgoing = (
        jnp.zeros((experts * capacity, width), jnp.bfloat16)
        .at[position]
        .set(jnp.repeat(normed, TOP, axis=0))
    )
    outgoing = outgoing.reshape(experts, capacity, width)
    hidden_units = w_down.shape[1]
    received = lax.all_to_all(outgoing, ("seq", "exp"), split_axis=0, concat_axis=0, tiled=True)
    sources, items, columns = received.shape
    flat_rows = received.reshape(sources * items, columns)
    both = jnp.dot(flat_rows, w_gate_up[0], preferred_element_type=jnp.float32)
    hidden = (jax.nn.silu(both[:, :hidden_units]) * both[:, hidden_units:]).astype(jnp.bfloat16)
    result = jnp.dot(hidden, w_down[0], preferred_element_type=jnp.float32).astype(jnp.bfloat16)
    processed = result.reshape(sources, items, columns)
    returned = lax.all_to_all(
        processed, ("seq", "exp"), split_axis=0, concat_axis=0, tiled=True
    ).reshape(experts * capacity, width)
    picked = returned[position].astype(jnp.float32).reshape(node_dev, TOP, width)
    expert_sum = jnp.sum(picked * gates[0][:, :, None], axis=1)
    return (mixed + expert_sum).astype(jnp.bfloat16)[None]


def solution(mesh):
    in_specs = (
        P(("sub", "exp"), "seq", None),
        P(("sub", "exp"), None, None),
        P("exp", "seq"),
        P("seq", "exp"),
        P(),
        P(("sub", "exp"), "seq", None),
        P(("sub", "exp"), "seq", None),
        P(("seq", "exp"), None, None),
        P(("seq", "exp"), None, None),
    )
    out_specs = P(("sub", "exp"), "seq", None)
    return jax.shard_map(
        per_device, mesh=mesh, in_specs=in_specs, out_specs=out_specs, check_vma=False
    )
```

profile of v0, /device:TPU:24, one launch (start us, length us, event | category | flops | bytes accessed | tf_op | source)
XLA Modules:
  0.0 382.8 jit_solution(14159090257780799350)
XLA Ops:
  6.5 0.0 copy-start
  6.5 0.0 all-gather.5.cloned.1.call-start
  6.5 0.7 all-gather.5.cloned.1.call-update
  7.3 1.1 copy.33
  8.3 97.1 %all-gather.5.cloned.1.call-done = bf16[8192,384]{1,0:T(8,128)(2,1)} async-done(((bf16[128,384]{1,0:T(8,128)(2,1)}), bf16[8192,384]{1,0:T(8,128)(2,1)}) %all-gather.5.cloned.1.call-update) | async-done | bytes 6291472 | tf_op jit(solution)/shard_map/all_gather | solution.py:22
  105.4 5.2 %bitcast_convert_fusion = bf16[192,8,384]{2,0,1:T(8,128)(2,1)} fusion(bf16[8,8,128,384]{3,2,1,0:T(8,128)(2,1)} %bitcast.99, bf16[192,8,128]{2,1,0:T(8,128)(2,1)S(1)} %bitcast.103), kind=kOutput, calls=%fused_computation.28 | convolution fusion | flops 1208549376 | bytes 7864320 | tf_op jit(solution)/shard_map/nek,sekc->nsc/dot_general | solution.py:26
  110.7 6.1 %all-to-all-start = ((bf16[192,8,384]{2,0,1:T(8,128)(2,1)}), bf16[192,8,384]{2,0,1:T(8,128)(2,1)S(1)}, u32[]{:S(2)}, u32[]{:S(2)}) async-start(bf16[192,8,384]{2,0,1:T(8,128)(2,1)} %bitcast_convert_fusion), calls=%async_computation | async-start | bytes 2359296 | tf_op jit(solution)/shard_map/all_to_all | solution.py:33
  116.7 0.0 all-gather.7.cloned.1.call-start
  116.7 0.7 all-gather.7.cloned.1.call-update
  117.5 0.0 copy-done.4
  117.5 0.1 copy.23
  117.6 0.1 eq.29
  117.7 0.1 eq.25
  117.9 0.0 copy-done.5
  117.9 0.1 broadcast_in_dim.65
  118.1 26.0 %all-to-all-done = bf16[192,8,384]{2,0,1:T(8,128)(2,1)S(1)} async-done(((bf16[192,8,384]{2,0,1:T(8,128)(2,1)}), bf16[192,8,384]{2,0,1:T(8,128)(2,1)S(1)}, u32[]{:S(2)}, u32[]{:S(2)}) %all-to-all-start) | async-done | bytes 1179680 | tf_op jit(solution)/shard_map/all_to_all | solution.py:33
  144.1 2.0 copy.18
  146.1 2.9 reshape.112
  149.0 1.1 slice_bitcast_fusion
  150.1 28.0 %while.12 = (s32[]{:T(128)}, bf16[3,512,2,64]{1,3,2,0:T(8,128)(2,1)}, s32[3]{0:T(128)S(1)}, pred[12,1536]{1,0:T(8,128)(4,1)S(1)}, bf16[1536,2,64]{0,2,1:T(8,128)...) while((s32[]{:T(128)}, ...), condition=%wide.region_3.4_spmd, body=%wide.region_0.3_spmd.sunk | while | flops 618205184 | bytes 5532574 | solution.py:60
  150.1 0.6 dynamic_slice.40
  151.3 0.2 broadcast_in_dim.104
  151.5 3.5 fusion.73
  155.0 4.4 %fusion.74 = bf16[3,512,2,64]{1,3,2,0:T(8,128)(2,1)} fusion(bf16[3,512,2,64]{1,3,2,0:T(8,128)(2,1)} %get-tuple-element.174, s32[]{:T(128)} %get-tuple-element.173, bf16[1536,2,64]{0,2,1:T(8,128)(2,1)S(1)} %copy-done.3, f32[2,512]{1,0:T(2,128)S(1)} %fusion.73, pred[512,1536]{1,0:T(8,128)(4,1)S(1)} %bitcast.97, ...), kind=kOutput, calls=%fused_computation.13.clone.1 | convolution fusion | flops 410585600 | bytes 1839620 | tf_op jit(solution)/shard_map/while/body/eval_jaxpr/hqk,khd->qhd/dot_general | solution.py:56
  159.4 0.6 dynamic_slice.40
  160.6 0.2 broadcast_in_dim.104
  160.9 0.0 copy-start.3
  160.9 3.5 fusion.73
  164.4 4.4 %fusion.74 = bf16[3,512,2,64]{1,3,2,0:T(8,128)(2,1)} fusion(bf16[3,512,2,64]{1,3,2,0:T(8,128)(2,1)} %get-tuple-element.174, s32[]{:T(128)} %get-tuple-element.173, bf16[1536,2,64]{0,2,1:T(8,128)(2,1)S(1)} %copy-done.3, f32[2,512]{1,0:T(2,128)S(1)} %fusion.73, pred[512,1536]{1,0:T(8,128)(4,1)S(1)} %bitcast.97, ...), kind=kOutput, calls=%fused_computation.13.clone.1 | convolution fusion | flops 410585600 | bytes 1839620 | tf_op jit(solution)/shard_map/while/body/eval_jaxpr/hqk,khd->qhd/dot_general | solution.py:56
  168.8 0.6 dynamic_slice.40
  170.0 0.2 broadcast_in_dim.104
  170.2 3.5 fusion.73
  173.7 4.4 %fusion.74 = bf16[3,512,2,64]{1,3,2,0:T(8,128)(2,1)} fusion(bf16[3,512,2,64]{1,3,2,0:T(8,128)(2,1)} %get-tuple-element.174, s32[]{:T(128)} %get-tuple-element.173, bf16[1536,2,64]{0,2,1:T(8,128)(2,1)S(1)} %copy-done.3, f32[2,512]{1,0:T(2,128)S(1)} %fusion.73, pred[512,1536]{1,0:T(8,128)(4,1)S(1)} %bitcast.97, ...), kind=kOutput, calls=%fused_computation.13.clone.1 | convolution fusion | flops 410585600 | bytes 1839620 | tf_op jit(solution)/shard_map/while/body/eval_jaxpr/hqk,khd->qhd/dot_general | solution.py:56
  178.1 2.2 copy.28
  180.3 1.1 reshape.145
  181.4 8.0 %all-to-all-start.1 = ((bf16[8,192,128]{2,1,0:T(8,128)(2,1)}), bf16[8,192,128]{2,1,0:T(8,128)(2,1)S(1)}, u32[]{:S(2)}, u32[]{:S(2)}) async-start(bf16[8,192,128]{2,1,0:T(8,128)(2,1)} %reshape.145), calls=%async_computation.1 | async-start | bytes 786432 | tf_op jit(solution)/shard_map/all_to_all | solution.py:62
  189.4 0.9 reduce-window.6
  190.3 0.2 slice_reduce_fusion
  190.6 0.1 copy.22
  190.7 0.1 mul.72
  190.9 0.1 fusion.48
  191.0 16.6 %all-gather.7.cloned.1.call-done = bf16[8192,128]{1,0:T(8,128)(2,1)} async-done(((bf16[128,128]{1,0:T(8,128)(2,1)}), bf16[8192,128]{1,0:T(8,128)(2,1)}) %all-gather.7.cloned.1.call-update) | async-done | bytes 2097168 | tf_op jit(solution)/shard_map/all_gather | solution.py:23
  207.6 4.0 %copy.21 = bf16[8,8,128,128]{2,3,1,0:T(8,128)(2,1)} copy(bf16[8,8,128,128]{3,2,1,0:T(8,128)(2,1)} %bitcast.101) | data formatting | bytes 4194304 | tf_op jit(solution)/shard_map/reshape | solution.py:63
  211.6 0.0 all-to-all-done.1
  211.6 0.7 copy-done.2
  212.3 2.7 multiply_reduce_fusion.1
  215.0 0.1 multiply_convert_fusion
  215.2 1.3 broadcast_in_dim.69
  216.5 3.0 reshape.134
  219.4 4.0 %scatter_custom_fusion = bf16[768,1024]{1,0:T(8,128)(2,1)} fusion(s32[384]{0:T(512)S(1)} %fusion.50, bf16[384,1024]{1,0:T(8,128)(2,1)} %reshape.134, bf16[]{:T(256)} %constant.96.clone.1), kind=kCustom, calls=%fused_computation.42 | custom fusion | bytes 1573376 | tf_op jit(solution)/shard_map/scatter | solution.py:82
  223.4 3.6 reshape.116
  227.0 59.8 %all_to_all.39 = bf16[64,12,1024]{2,1,0:T(8,128)(2,1)} all-to-all(bf16[64,12,1024]{2,1,0:T(8,128)(2,1)} %reshape.116), channel_id=1, replica_groups=mesh['sub'=8,'seq'=8,'exp'=8] {'seq','exp'}, dimensions={0} | all-to-all | bytes 3145728 | tf_op jit(solution)/shard_map/all_to_all | solution.py:86
  286.8 3.6 reshape.117
  290.4 3.3 fusion.33
  293.7 2.2 convolution_convert_fusion
  295.9 3.6 reshape.118
  299.5 7.7 %all-to-all-start.3 = ((bf16[64,12,1024]{2,1,0:T(8,128)(2,1)}), bf16[64,12,1024]{2,1,0:T(8,128)(2,1)}, u32[]{:S(2)}, u32[]{:S(2)}) async-start(bf16[64,12,1024]{2,1,0:T(8,128)(2,1)} %reshape.118), calls=%async_computation.3 | async-start | bytes 4194304 | tf_op jit(solution)/shard_map/all_to_all | solution.py:93
  307.2 0.1 copy.26
  307.3 52.9 %all-to-all-done.3 = bf16[64,12,1024]{2,1,0:T(8,128)(2,1)} async-done(((bf16[64,12,1024]{2,1,0:T(8,128)(2,1)}), bf16[64,12,1024]{2,1,0:T(8,128)(2,1)}, u32[]{:S(2)}, u32[]{:S(2)}) %all-to-all-start.3) | async-done | bytes 1572896 | tf_op jit(solution)/shard_map/all_to_all | solution.py:93
  360.2 3.6 reshape.119
  363.8 5.0 %gather_fusion = bf16[384,1024]{1,0:T(8,128)(2,1)} fusion(bf16[768,1024]{1,0:T(8,128)(2,1)} %reshape.119, s32[1024]{0:T(1024)S(1)} %pad_clamp_fusion), kind=kCustom, calls=%fused_computation | custom fusion | bytes 1574400 | tf_op jit(solution)/shard_map/gather | solution.py:96
  368.7 3.0 reshape.121
  371.7 3.4 multiply_reduce_fusion
  375.1 0.8 fusion.42
  (32 shorter events, 0.2 us)
Async XLA Ops:
  6.5 283.9 %copy-start = (bf16[1,1024,1024]{2,1,0:T(8,128)(2,1)S(1)}, bf16[1,1024,1024]{2,1,0:T(8,128)(2,1)}, u32[]{:S(2)}) copy-start(bf16[1,1024,1024]{2,1,0:T(8,128)(2,1)} %param.18) | copy-start | bytes 6291460
  6.5 98.9 %all-gather.5.cloned.1.call-start = ((), (), s32[]{:S(2)}) async-start(), calls=%async_computation.4 | async-start | bytes 6389760 | tf_op jit(solution)/shard_map/all_gather | solution.py:22
  110.7 6.8 %copy-start.4 = (s32[1,192,2]{1,2,0:T(2,128)S(1)}, s32[1,192,2]{1,2,0:T(2,128)}, u32[]{:S(2)}) copy-start(s32[1,192,2]{1,2,0:T(2,128)} %param.16) | copy-start | bytes 4612
  110.7 7.2 %copy-start.5 = (s32[1,12,12]{2,0,1:T(1,128)S(1)}, s32[1,12,12]{2,0,1:T(1,128)}, u32[]{:S(2)}) copy-start(s32[1,12,12]{2,0,1:T(1,128)} %param.12) | copy-start | bytes 1732
  110.7 33.4 %all-to-all-start = ((bf16[192,8,384]{2,0,1:T(8,128)(2,1)}), bf16[192,8,384]{2,0,1:T(8,128)(2,1)S(1)}, u32[]{:S(2)}, u32[]{:S(2)}) async-start(bf16[192,8,384]{2,0,1:T(8,128)(2,1)} %bitcast_convert_fusion), calls=%async_computation | async-start | bytes 2359296 | tf_op jit(solution)/shard_map/all_to_all | solution.py:33
  116.7 90.9 %all-gather.7.cloned.1.call-start = ((), (), s32[]{:S(2)}) async-start(), calls=%async_computation.5 | async-start | bytes 2129920 | tf_op jit(solution)/shard_map/all_gather | solution.py:23
  151.5 3.5 copy-start.3
  160.9 3.5 copy-start.3
  170.2 3.5 copy-start.3
  181.4 30.2 %all-to-all-start.1 = ((bf16[8,192,128]{2,1,0:T(8,128)(2,1)}), bf16[8,192,128]{2,1,0:T(8,128)(2,1)S(1)}, u32[]{:S(2)}, u32[]{:S(2)}) async-start(bf16[8,192,128]{2,1,0:T(8,128)(2,1)} %reshape.145), calls=%async_computation.1 | async-start | bytes 786432 | tf_op jit(solution)/shard_map/all_to_all | solution.py:62
  207.6 4.7 %copy-start.1 = (bf16[1,192,1024]{2,1,0:T(8,128)(2,1)S(1)}, bf16[1,192,1024]{2,1,0:T(8,128)(2,1)}, u32[]{:S(2)}) copy-start(bf16[1,192,1024]{2,1,0:T(8,128)(2,1)} %param.11) | copy-start | bytes 1179652
  211.6 3.4 copy-start.6
  211.6 0.7 copy-start.2
  290.4 3.3 copy-start.8
  299.5 7.7 %copy-start.7 = (f32[1,192,2]{1,2,0:T(2,128)S(1)}, f32[1,192,2]{1,2,0:T(2,128)}, u32[]{:S(2)}) copy-start(f32[1,192,2]{1,2,0:T(2,128)} %param.17) | copy-start | bytes 4612
  299.5 60.7 %all-to-all-start.3 = ((bf16[64,12,1024]{2,1,0:T(8,128)(2,1)}), bf16[64,12,1024]{2,1,0:T(8,128)(2,1)}, u32[]{:S(2)}, u32[]{:S(2)}) async-start(bf16[64,12,1024]{2,1,0:T(8,128)(2,1)} %reshape.118), calls=%async_computation.3 | async-start | bytes 4194304 | tf_op jit(solution)/shard_map/all_to_all | solution.py:93
Sparse Core Ops, SparseCore 0:
  10.4 94.9 all-gather.4
  120.6 86.9 all-gather.6
where the time goes:
time: 384 us; the launch traced here: 383 us
  waiting for transfers between devices  194 us (51%)
  blocking collectives  59.8 us (16%)
  local copies, waits for them, and re-layouts  49.3 us (13%)
  matrix products  37 us (10%)
  starting transfers between devices  21.8 us (6%)
  between operations  13.6 us (4%)
  other arithmetic  5.53 us (1%)
    all_gather x1, waiting for transfers between devices, per_device(): lax.all_gather(w_qkv[None], ('seq', 'exp'), axis=0, tiled=True)  97.1 us
    all_to_all x1, blocking collectives, per_device(): lax.all_to_all(outgoing, ('seq', 'exp'), split_axis=0, concat_axis=0, til...  59.8 us
    all_to_all x1, waiting for transfers between devices, per_device(): lax.all_to_all(processed, ('seq', 'exp'), split_axis=0, concat_axis=0, ti...  52.9 us
    all_to_all x1, waiting for transfers between devices, per_device(): lax.all_to_all(local_proj, 'seq', split_axis=1, concat_axis=0, tiled=True)  26 us
    all_gather x1, waiting for transfers between devices, per_device(): lax.all_gather(w_out[None], ('seq', 'exp'), axis=0, tiled=True)  16.6 us
    dot_general x3, matrix products, attend(): jnp.einsum('hqk,khd->qhd', probs, values, preferred_element_type=jnp.floa...  13.2 us
    sub x3, matrix products, attend(): weights = jnp.exp(scores - top)  10.4 us
    all_to_all x1, starting transfers between devices, per_device(): lax.all_to_all(attended, 'seq', split_axis=0, concat_axis=1, tiled=True)  8.03 us
  transfers between devices with their start and end apart: 5, of which 4 were waited for; matrix products, arithmetic and copies ran while one was open for 11% of the time, Pallas kernels for 0%

commit v1 on v0

--- a/solution.py
+++ b/solution.py
@@ -18,9 +18,17 @@
     exp_count = lax.axis_size("exp")
     experts = seq_count * exp_count * w_gate_up.shape[0]
     head_cols = w_qkv.shape[1]
+
+    def fill_columns(u_in):
+        arr_now = jax.lax.axis_size(("seq", "exp"))
+        response = jnp.stack([u_in] * arr_now, axis=0)
+        s_next = jax.lax.all_to_all(response, axis_name=("seq", "exp"), split_axis=0, concat_axis=0)
+        v_next = jnp.concatenate(s_next, axis=0)
+        return v_next
+
     qkv_all, out_all = (
         lax.all_gather(w_qkv[None], ("seq", "exp"), axis=0, tiled=True),
-        lax.all_gather(w_out[None], ("seq", "exp"), axis=0, tiled=True),
+        fill_columns(w_out[None]),
     )
     qkv_tiles = qkv_all.reshape(seq_count, exp_count, w_qkv.shape[0], head_cols)
     local_proj = jnp.einsum(

time: 384 us -> 405 us (1.055)
  waiting for transfers between devices: 194 us -> 204 us
  starting transfers between devices: 21.8 us -> 29 us
  blocking collectives: 59.8 us -> 64.8 us
    all_to_all x0 -> x1, waiting for transfers between devices: none -> 19.6 us  [fill_columns(): jax.lax.all_to_all(response, axis_name=('seq', 'exp'), split_axis=0, conc...]
    all_gather x1 -> x0, waiting for transfers between devices: 16.6 us -> none  [per_device(): lax.all_gather(w_out[None], ('seq', 'exp'), axis=0, tiled=True)]
    all_to_all x0 -> x1, starting transfers between devices: none -> 9.72 us  [fill_columns(): jax.lax.all_to_all(response, axis_name=('seq', 'exp'), split_axis=0, conc...]
    all_to_all x1, waiting for transfers between devices: 0.01 us -> 7.18 us  [per_device(): lax.all_to_all(attended, 'seq', split_axis=0, concat_axis=1, tiled=True)]
    all_to_all x1, blocking collectives: 59.8 us -> 64.8 us  [per_device(): lax.all_to_all(outgoing, ('seq', 'exp'), split_axis=0, concat_axis=0, til...]
  transfers between devices with their start and end apart: 5 -> 5, of which waited for: 4 -> 5; matrix products, arithmetic and copies ran while one was open for 11% -> 10% of each run, Pallas kernels for 0% -> 0%
where the time goes in v1:
time: 405 us; the launch traced here: 403 us
  waiting for transfers between devices  204 us (50%)
  blocking collectives  64.8 us (16%)
  local copies, waits for them, and re-layouts  47.3 us (12%)
  matrix products  37 us (9%)
  starting transfers between devices  29 us (7%)
  between operations  13.6 us (3%)
  other arithmetic  5.53 us (1%)
    all_gather x1, waiting for transfers between devices, per_device(): lax.all_gather(w_qkv[None], ('seq', 'exp'), axis=0, tiled=True)  97.1 us
    all_to_all x1, blocking collectives, per_device(): lax.all_to_all(outgoing, ('seq', 'exp'), split_axis=0, concat_axis=0, til...  64.8 us
    all_to_all x1, waiting for transfers between devices, per_device(): lax.all_to_all(processed, ('seq', 'exp'), split_axis=0, concat_axis=0, ti...  52.5 us
    all_to_all x1, waiting for transfers between devices, per_device(): lax.all_to_all(local_proj, 'seq', split_axis=1, concat_axis=0, tiled=True)  27 us
    all_to_all x1, waiting for transfers between devices, fill_columns(): jax.lax.all_to_all(response, axis_name=('seq', 'exp'), split_axis=0, conc...  19.6 us
    dot_general x3, matrix products, attend(): jnp.einsum('hqk,khd->qhd', probs, values, preferred_element_type=jnp.floa...  13.2 us
    sub x3, matrix products, attend(): weights = jnp.exp(scores - top)  10.4 us
    all_to_all x1, starting transfers between devices, fill_columns(): jax.lax.all_to_all(response, axis_name=('seq', 'exp'), split_axis=0, conc...  9.72 us
  transfers between devices with their start and end apart: 5, of which 5 were waited for; matrix products, arithmetic and copies ran while one was open for 10% of the time, Pallas kernels for 0%

profile of v1, /device:TPU:24, one launch (start us, length us, event | category | flops | bytes accessed | tf_op | source)
XLA Modules:
  0.0 403.3 jit_solution(16632583228420357786)
XLA Ops:
  6.5 0.0 copy-start
  6.5 0.0 all-gather.3.cloned.1.call-start
  6.5 0.7 all-gather.3.cloned.1.call-update
  7.3 1.1 copy.43
  8.3 97.1 %all-gather.3.cloned.1.call-done = bf16[8192,384]{1,0:T(8,128)(2,1)} async-done(((bf16[128,384]{1,0:T(8,128)(2,1)}), bf16[8192,384]{1,0:T(8,128)(2,1)}) %all-gather.3.cloned.1.call-update) | async-done | bytes 6291472 | tf_op jit(solution)/shard_map/all_gather | solution.py:30
  105.4 5.2 %bitcast_convert_fusion = bf16[192,8,384]{2,0,1:T(8,128)(2,1)} fusion(bf16[8,8,128,384]{3,2,1,0:T(8,128)(2,1)} %bitcast.99, bf16[192,8,128]{2,1,0:T(8,128)(2,1)S(1)} %bitcast.102), kind=kOutput, calls=%fused_computation.28 | convolution fusion | flops 1208549376 | bytes 7864320 | tf_op jit(solution)/shard_map/nek,sekc->nsc/dot_general | solution.py:34
  110.7 6.1 %all-to-all-start = ((bf16[192,8,384]{2,0,1:T(8,128)(2,1)}), bf16[192,8,384]{2,0,1:T(8,128)(2,1)S(1)}, u32[]{:S(2)}, u32[]{:S(2)}) async-start(bf16[192,8,384]{2,0,1:T(8,128)(2,1)} %bitcast_convert_fusion), calls=%async_computation | async-start | bytes 2359296 | tf_op jit(solution)/shard_map/all_to_all | solution.py:41
  116.7 0.0 copy-done.4
  116.7 0.1 copy.31
  116.8 27.0 %all-to-all-done = bf16[192,8,384]{2,0,1:T(8,128)(2,1)S(1)} async-done(((bf16[192,8,384]{2,0,1:T(8,128)(2,1)}), bf16[192,8,384]{2,0,1:T(8,128)(2,1)S(1)}, u32[]{:S(2)}, u32[]{:S(2)}) %all-to-all-start) | async-done | bytes 1179680 | tf_op jit(solution)/shard_map/all_to_all | solution.py:41
  143.8 1.8 stack.3
  145.6 9.7 %all-to-all-start.2 = ((bf16[64,1,128,128]{2,3,1,0:T(8,128)(2,1)}), bf16[64,1,128,128]{2,3,1,0:T(8,128)(2,1)}, u32[]{:S(2)}, u32[]{:S(2)}) async-start(bf16[64,1,128,128]{2,3,1,0:T(8,128)(2,1)} %stack.3), calls=%async_computation.2 | async-start | bytes 4194304 | tf_op jit(solution)/shard_map/all_to_all | solution.py:25
  155.3 0.0 copy-done.5
  155.3 0.1 copy.33
  155.5 0.1 eq.29
  155.6 0.1 eq.25
  155.8 0.1 broadcast_in_dim.62
  155.9 2.1 copy.28
  158.0 2.9 reshape.111
  160.9 1.0 slice_bitcast_fusion
  162.0 28.1 %while.12 = (s32[]{:T(128)}, bf16[3,512,2,64]{1,3,2,0:T(8,128)(2,1)}, s32[3]{0:T(128)S(1)}, pred[12,1536]{1,0:T(8,128)(4,1)S(1)}, bf16[1536,2,64]{0,2,1:T(8,128)...) while((s32[]{:T(128)}, ...), condition=%wide.region_3.4_spmd, body=%wide.region_0.3_spmd.sunk | while | flops 618205184 | bytes 5532574 | solution.py:68
  162.0 0.6 dynamic_slice.40
  163.2 0.2 broadcast_in_dim.100
  163.4 3.5 fusion.73
  166.9 4.4 %fusion.74 = bf16[3,512,2,64]{1,3,2,0:T(8,128)(2,1)} fusion(bf16[3,512,2,64]{1,3,2,0:T(8,128)(2,1)} %get-tuple-element.174, s32[]{:T(128)} %get-tuple-element.173, bf16[1536,2,64]{0,2,1:T(8,128)(2,1)S(1)} %copy-done.3, f32[2,512]{1,0:T(2,128)S(1)} %fusion.73, pred[512,1536]{1,0:T(8,128)(4,1)S(1)} %bitcast.98, ...), kind=kOutput, calls=%fused_computation.13.clone.1 | convolution fusion | flops 410585600 | bytes 1839620 | tf_op jit(solution)/shard_map/while/body/eval_jaxpr/hqk,khd->qhd/dot_general | solution.py:64
  171.3 0.6 dynamic_slice.40
  172.6 0.2 broadcast_in_dim.100
  172.8 3.5 fusion.73
  176.3 4.4 %fusion.74 = bf16[3,512,2,64]{1,3,2,0:T(8,128)(2,1)} fusion(bf16[3,512,2,64]{1,3,2,0:T(8,128)(2,1)} %get-tuple-element.174, s32[]{:T(128)} %get-tuple-element.173, bf16[1536,2,64]{0,2,1:T(8,128)(2,1)S(1)} %copy-done.3, f32[2,512]{1,0:T(2,128)S(1)} %fusion.73, pred[512,1536]{1,0:T(8,128)(4,1)S(1)} %bitcast.98, ...), kind=kOutput, calls=%fused_computation.13.clone.1 | convolution fusion | flops 410585600 | bytes 1839620 | tf_op jit(solution)/shard_map/while/body/eval_jaxpr/hqk,khd->qhd/dot_general | solution.py:64
  180.7 0.6 dynamic_slice.40
  181.9 0.2 broadcast_in_dim.100
  182.1 3.5 fusion.73
  185.6 4.4 %fusion.74 = bf16[3,512,2,64]{1,3,2,0:T(8,128)(2,1)} fusion(bf16[3,512,2,64]{1,3,2,0:T(8,128)(2,1)} %get-tuple-element.174, s32[]{:T(128)} %get-tuple-element.173, bf16[1536,2,64]{0,2,1:T(8,128)(2,1)S(1)} %copy-done.3, f32[2,512]{1,0:T(2,128)S(1)} %fusion.73, pred[512,1536]{1,0:T(8,128)(4,1)S(1)} %bitcast.98, ...), kind=kOutput, calls=%fused_computation.13.clone.1 | convolution fusion | flops 410585600 | bytes 1839620 | tf_op jit(solution)/shard_map/while/body/eval_jaxpr/hqk,khd->qhd/dot_general | solution.py:64
  190.0 2.2 copy.38
  192.3 1.1 reshape.141
  193.4 19.6 %all-to-all-done.2 = bf16[64,1,128,128]{2,3,1,0:T(8,128)(2,1)} async-done(((bf16[64,1,128,128]{2,3,1,0:T(8,128)(2,1)}), bf16[64,1,128,128]{2,3,1,0:T(8,128)(2,1)}, u32[]{:S(2)}, u32[]{:S(2)}) %all-to-all-start.2) | async-done | bytes 2097184 | tf_op jit(solution)/shard_map/all_to_all | solution.py:25
  213.0 5.1 %all-to-all-start.1 = ((bf16[8,192,128]{2,1,0:T(8,128)(2,1)}), bf16[8,192,128]{2,1,0:T(8,128)(2,1)S(1)}, u32[]{:S(2)}, u32[]{:S(2)}) async-start(bf16[8,192,128]{2,1,0:T(8,128)(2,1)} %reshape.141), calls=%async_computation.1 | async-start | bytes 786432 | tf_op jit(solution)/shard_map/all_to_all | solution.py:70
  218.1 0.9 reduce-window.6
  219.0 0.2 slice_reduce_fusion
  219.3 0.1 copy.32
  219.4 0.1 mul.72
  219.6 0.1 fusion.48
  219.7 7.2 %all-to-all-done.1 = bf16[8,192,128]{2,1,0:T(8,128)(2,1)S(1)} async-done(((bf16[8,192,128]{2,1,0:T(8,128)(2,1)}), bf16[8,192,128]{2,1,0:T(8,128)(2,1)S(1)}, u32[]{:S(2)}, u32[]{:S(2)}) %all-to-all-start.1) | async-done | bytes 393248 | tf_op jit(solution)/shard_map/all_to_all | solution.py:70
  226.9 0.7 copy-done.2
  227.6 0.0 copy-done.1
  227.6 2.7 multiply_reduce_fusion.1
  230.3 0.1 multiply_convert_fusion
  230.4 1.3 broadcast_in_dim.65
  231.8 3.0 reshape.132
  234.7 4.0 scatter_custom_fusion
  238.7 3.6 reshape.114
  242.3 64.8 %all_to_all.44 = bf16[64,12,1024]{2,1,0:T(8,128)(2,1)} all-to-all(bf16[64,12,1024]{2,1,0:T(8,128)(2,1)} %reshape.114), channel_id=1, replica_groups=mesh['sub'=8,'seq'=8,'exp'=8] {'seq','exp'}, dimensions={0} | all-to-all | bytes 3145728 | tf_op jit(solution)/shard_map/all_to_all | solution.py:94
  307.1 3.6 reshape.115
  310.8 3.3 fusion.33
  314.1 2.2 convolution_convert_fusion
  316.2 3.6 reshape.116
  319.8 8.1 %all-to-all-start.4 = ((bf16[64,12,1024]{2,1,0:T(8,128)(2,1)}), bf16[64,12,1024]{2,1,0:T(8,128)(2,1)}, u32[]{:S(2)}, u32[]{:S(2)}) async-start(bf16[64,12,1024]{2,1,0:T(8,128)(2,1)} %reshape.116), calls=%async_computation.4 | async-start | bytes 4194304 | tf_op jit(solution)/shard_map/all_to_all | solution.py:101
  328.0 0.1 copy.36
  328.1 52.5 %all-to-all-done.4 = bf16[64,12,1024]{2,1,0:T(8,128)(2,1)} async-done(((bf16[64,12,1024]{2,1,0:T(8,128)(2,1)}), bf16[64,12,1024]{2,1,0:T(8,128)(2,1)}, u32[]{:S(2)}, u32[]{:S(2)}) %all-to-all-start.4) | async-done | bytes 1572896 | tf_op jit(solution)/shard_map/all_to_all | solution.py:101
  380.6 3.6 reshape.117
  384.2 5.0 %gather_fusion = bf16[384,1024]{1,0:T(8,128)(2,1)} fusion(bf16[768,1024]{1,0:T(8,128)(2,1)} %reshape.117, s32[1024]{0:T(1024)S(1)} %pad_clamp_fusion), kind=kCustom, calls=%fused_computation | custom fusion | bytes 1574400 | tf_op jit(solution)/shard_map/gather | solution.py:104
  389.2 3.0 reshape.119
  392.2 3.4 multiply_reduce_fusion
  395.6 0.8 fusion.42
  (34 shorter events, 0.2 us)
Async XLA Ops:
  6.5 304.2 %copy-start = (bf16[1,1024,1024]{2,1,0:T(8,128)(2,1)S(1)}, bf16[1,1024,1024]{2,1,0:T(8,128)(2,1)}, u32[]{:S(2)}) copy-start(bf16[1,1024,1024]{2,1,0:T(8,128)(2,1)} %param.18) | copy-start | bytes 6291460
  6.5 98.9 %all-gather.3.cloned.1.call-start = ((), (), s32[]{:S(2)}) async-start(), calls=%async_computation.5 | async-start | bytes 6389760 | tf_op jit(solution)/shard_map/all_gather | solution.py:30
  110.7 6.1 %copy-start.4 = (bf16[128,128]{1,0:T(8,128)(2,1)S(1)}, bf16[128,128]{1,0:T(8,128)(2,1)}, u32[]{:S(2)}) copy-start(bf16[128,128]{1,0:T(8,128)(2,1)} %param.14) | copy-start | bytes 98308
  110.7 33.1 %all-to-all-start = ((bf16[192,8,384]{2,0,1:T(8,128)(2,1)}), bf16[192,8,384]{2,0,1:T(8,128)(2,1)S(1)}, u32[]{:S(2)}, u32[]{:S(2)}) async-start(bf16[192,8,384]{2,0,1:T(8,128)(2,1)} %bitcast_convert_fusion), calls=%async_computation | async-start | bytes 2359296 | tf_op jit(solution)/shard_map/all_to_all | solution.py:41
  145.6 9.7 %copy-start.5 = (s32[1,192,2]{1,2,0:T(2,128)S(1)}, s32[1,192,2]{1,2,0:T(2,128)}, u32[]{:S(2)}) copy-start(s32[1,192,2]{1,2,0:T(2,128)} %param.16) | copy-start | bytes 4612
  145.6 10.2 %copy-start.6 = (s32[1,12,12]{2,0,1:T(1,128)S(1)}, s32[1,12,12]{2,0,1:T(1,128)}, u32[]{:S(2)}) copy-start(s32[1,12,12]{2,0,1:T(1,128)} %param.12) | copy-start | bytes 1732
  145.6 67.4 %all-to-all-start.2 = ((bf16[64,1,128,128]{2,3,1,0:T(8,128)(2,1)}), bf16[64,1,128,128]{2,3,1,0:T(8,128)(2,1)}, u32[]{:S(2)}, u32[]{:S(2)}) async-start(bf16[64,1,128,128]{2,3,1,0:T(8,128)(2,1)} %stack.3), calls=%async_computation.2 | async-start | bytes 4194304 | tf_op jit(solution)/shard_map/all_to_all | solution.py:25
  163.4 3.5 copy-start.3
  172.8 3.5 copy-start.3
  182.1 3.5 copy-start.3
  190.0 37.6 %copy-start.1 = (bf16[1,192,1024]{2,1,0:T(8,128)(2,1)S(1)}, bf16[1,192,1024]{2,1,0:T(8,128)(2,1)}, u32[]{:S(2)}) copy-start(bf16[1,192,1024]{2,1,0:T(8,128)(2,1)} %param.11) | copy-start | bytes 1179652
  213.0 13.9 %all-to-all-start.1 = ((bf16[8,192,128]{2,1,0:T(8,128)(2,1)}), bf16[8,192,128]{2,1,0:T(8,128)(2,1)S(1)}, u32[]{:S(2)}, u32[]{:S(2)}) async-start(bf16[8,192,128]{2,1,0:T(8,128)(2,1)} %reshape.141), calls=%async_computation.1 | async-start | bytes 786432 | tf_op jit(solution)/shard_map/all_to_all | solution.py:70
  219.0 11.3 %copy-start.7 = (f32[1024]{0:T(1024)S(1)}, f32[1024]{0:T(1024)}, u32[]{:S(2)}) copy-start(f32[1024]{0:T(1024)} %param.15) | copy-start | bytes 12292
  226.9 0.7 copy-start.2
  310.8 3.3 copy-start.9
  319.8 8.2 %copy-start.8 = (f32[1,192,2]{1,2,0:T(2,128)S(1)}, f32[1,192,2]{1,2,0:T(2,128)}, u32[]{:S(2)}) copy-start(f32[1,192,2]{1,2,0:T(2,128)} %param.17) | copy-start | bytes 4612
  319.8 60.8 %all-to-all-start.4 = ((bf16[64,12,1024]{2,1,0:T(8,128)(2,1)}), bf16[64,12,1024]{2,1,0:T(8,128)(2,1)}, u32[]{:S(2)}, u32[]{:S(2)}) async-start(bf16[64,12,1024]{2,1,0:T(8,128)(2,1)} %reshape.116), calls=%async_computation.4 | async-start | bytes 4194304 | tf_op jit(solution)/shard_map/all_to_all | solution.py:101
Sparse Core Ops, SparseCore 0:
  10.4 94.9 all-gather.2
